TPU v7x, 128 devices: a whole 4x4x4 slice. The times are simulated.
128 devices in a mesh: req: 8 (over y, core), exp: 16 (over z, x).
Axes of the slice: x: 4, y: 4, z: 4, core: 2. Of those that a mesh axis runs over, the one named last changes fastest.
Arguments:
- hidden: bfloat16 [16384, 2560], P(('req', 'exp')), may hold values from -1.5 to 1.5
- queries: bfloat16 [16384, 1280], P(('req', 'exp')), may hold values from -100 to 100
- suffix_kv: bfloat16 [16384, 512], P(('req', 'exp')), may hold values from -24 to 24
- lengths: int32 [8, 4], P('req'), may hold values from 1 to 1024, 2048 in all within a row
- page_table: int32 [8, 4, 32], P('req'), may hold values from 0 to 55
- page_pool: bfloat16 [56, 128, 512], P('req'), may hold values from -24 to 24
- w_out: bfloat16 [1280, 2560], replicated, may hold values from -0.15625 to 0.15625
- w_router: bfloat16 [2560, 64], replicated, may hold values from -5 to 5
- routes: int32 [16384, 6], P(('req', 'exp')), may hold values from 0 to 63, all different within a row; in each aligned block of 128 rows (0 to 127, 128 to 255, ...) at most 15 rows name the same one
- w_gate: bfloat16 [128, 2560, 768], P(('req', 'exp')), may hold values from -0.125 to 0.125
- w_up: bfloat16 [128, 2560, 768], P(('req', 'exp')), may hold values from -0.125 to 0.125
- w_down: bfloat16 [128, 768, 2560], P(('req', 'exp')), may hold values from -0.4375 to 0.4375
Outputs:
- layer_out: bfloat16 [16384, 2560], P(('req', 'exp'))
Inputs may be any that keep to these rules, and one draw needn't show every extreme that they name: `lengths`: each row sums to 2048; its largest entry is exactly 1024. `page_table`: a page may appear in several prefixes and more than once in one. `routes`: the 6 experts of a token are distinct; among the rows of one device no expert is named more than 15 times, a bound that some block reaches.
All inputs are finite; a program needn't handle non-finite values.
Results may differ from a plain program's by a relative error of at most 0.022.
Values may be sent and summed in bfloat16 or wider, within the bound.
No kernel may reach another device: no remote copies, remote signals or barrier semaphores. Data moves between devices by JAX's collectives and lax.ppermute only.
A program may use at most 192 MiB of HBM per device.

v0:
```python
import math
import jax
import jax.numpy as jnp
from jax import lax
from jax.sharding import PartitionSpec as P

D = 2560
QUERY_HEADS = 10
KEY_VALUE_HEADS = 2
HEAD_SIZE = 128
TOP = 6
PAGE_TOKENS = 128
NEGATIVE_MASK = -1e30
EPS = 1e-06


def fold_scores(carry, query_matrix, key_rows, value_rows, weights):
    scores = jnp.einsum(
        "tgrd,kgd->tgrk", query_matrix, key_rows, preferred_element_type=jnp.float32
    ) * (1.0 / math.sqrt(HEAD_SIZE))
    running_maximum, grand_total, summed_output = carry
    live = weights[:, None, None, :] > 0
    fresh = jnp.maximum(running_maximum, jnp.max(jnp.where(live, scores, NEGATIVE_MASK), axis=-1))
    expo = jnp.where(live, jnp.exp(scores - fresh[..., None]), 0.0) * weights[:, None, None, :]
    decay = jnp.exp(running_maximum - fresh)
    grand_total = decay * grand_total + jnp.sum(expo, axis=-1)
    summed_output = decay[..., None] * summed_output + jnp.einsum(
        "tgrk,kgd->tgrd", expo.astype(jnp.bfloat16), value_rows, preferred_element_type=jnp.float32
    )
    return (fresh, grand_total, summed_output)


def empty_carry(token_count, request_groups):
    return (
        jnp.full((token_count, KEY_VALUE_HEADS, request_groups), NEGATIVE_MASK, jnp.float32),
        jnp.zeros((token_count, KEY_VALUE_HEADS, request_groups), jnp.float32),
        jnp.zeros((token_count, KEY_VALUE_HEADS, request_groups, HEAD_SIZE), jnp.float32),
    )


def on_device(
    hidden,
    queries,
    suffix_kv,
    lengths,
    page_table,
    page_pool,
    w_out,
    w_router,
    routes,
    w_gate,
    w_up,
    w_down,
):
    token_index = hidden.shape[0]
    row_width = KEY_VALUE_HEADS * HEAD_SIZE
    request_groups = QUERY_HEADS // KEY_VALUE_HEADS
    request_count = lax.axis_size("req")
    pool_per_shard = page_pool.shape[0]
    pool_all = pool_per_shard * request_count
    query_matrix = queries.reshape(token_index, KEY_VALUE_HEADS, request_groups, HEAD_SIZE)
    positions = lax.axis_index("exp") * token_index + jnp.arange(token_index, dtype=jnp.int32)
    lens = lengths[0]
    ends = jnp.cumsum(lens)
    starts = ends - lens
    req_of = jnp.sum((positions[:, None] >= ends[None, :]).astype(jnp.int32), axis=1)
    pick = req_of[:, None] == jnp.arange(lens.shape[0], dtype=jnp.int32)[None, :]
    first = jnp.sum(jnp.where(pick, starts[None, :], 0), axis=1)
    counts = jnp.sum(
        (page_table[0][:, :, None] == jnp.arange(pool_all, dtype=jnp.int32)[None, None, :]).astype(
            jnp.float32
        ),
        axis=1,
    )
    query_counts = jnp.dot(pick.astype(jnp.float32), counts, precision=lax.Precision.HIGHEST)
    query_total_set, every_count = (
        lax.all_gather(queries, "req", axis=0, tiled=True),
        lax.all_gather(query_counts.astype(jnp.bfloat16), "req", axis=0, tiled=True),
    )
    query_total_count = query_total_set.shape[0]
    local = lax.dynamic_slice_in_dim(
        every_count, lax.axis_index("req") * pool_per_shard, pool_per_shard, 1
    ).astype(jnp.float32)
    weights = jnp.repeat(local, PAGE_TOKENS, axis=1)
    flattened = page_pool.reshape(pool_per_shard * PAGE_TOKENS, 2 * row_width)
    key_rows = flattened[:, :row_width].reshape(
        pool_per_shard * PAGE_TOKENS, KEY_VALUE_HEADS, HEAD_SIZE
    )
    value_rows = flattened[:, row_width:].reshape(
        pool_per_shard * PAGE_TOKENS, KEY_VALUE_HEADS, HEAD_SIZE
    )
    running_maximum, grand_total, summed_output = fold_scores(
        empty_carry(query_total_count, request_groups),
        query_total_set.reshape(query_total_count, KEY_VALUE_HEADS, request_groups, HEAD_SIZE),
        key_rows,
        value_rows,
        weights,
    )
    peaks, totals, sums = (
        lax.all_to_all(
            running_maximum.reshape(request_count, token_index, KEY_VALUE_HEADS, request_groups),
            "req",
            split_axis=0,
            concat_axis=0,
            tiled=True,
        ),
        lax.all_to_all(
            grand_total.reshape(request_count, token_index, KEY_VALUE_HEADS, request_groups),
            "req",
            split_axis=0,
            concat_axis=0,
            tiled=True,
        ),
        lax.all_to_all(
            summed_output.reshape(
                request_count, token_index, KEY_VALUE_HEADS, request_groups, HEAD_SIZE
            ),
            "req",
            split_axis=0,
            concat_axis=0,
            tiled=True,
        ),
    )
    highest = jnp.max(peaks, axis=0)
    factor = jnp.exp(peaks - highest[None])
    carry = (highest, jnp.sum(factor * totals, axis=0), jnp.sum(factor[..., None] * sums, axis=0))
    segment = lax.all_gather(suffix_kv, "exp", axis=0, tiled=True)
    token_count = segment.shape[0]
    keypos = jnp.arange(token_count, dtype=jnp.int32)
    weights = (
        (keypos[None, :] <= positions[:, None]) & (keypos[None, :] >= first[:, None])
    ).astype(jnp.float32)
    key_rows = segment[:, :row_width].reshape(token_count, KEY_VALUE_HEADS, HEAD_SIZE)
    value_rows = segment[:, row_width:].reshape(token_count, KEY_VALUE_HEADS, HEAD_SIZE)
    running_maximum, grand_total, summed_output = fold_scores(
        carry, query_matrix, key_rows, value_rows, weights
    )
    attended = (
        (summed_output / grand_total[..., None])
        .reshape(token_index, QUERY_HEADS * HEAD_SIZE)
        .astype(jnp.bfloat16)
    )
    projected = jnp.dot(attended, w_out, preferred_element_type=jnp.float32)
    resid = lax.optimization_barrier((hidden.astype(jnp.float32) + projected).astype(jnp.bfloat16))
    resid_f = resid.astype(jnp.float32)
    normed = (resid_f * lax.rsqrt(jnp.mean(resid_f * resid_f, axis=1, keepdims=True) + EPS)).astype(
        jnp.bfloat16
    )
    n_experts = w_router.shape[1]
    logits = jnp.dot(normed, w_router, preferred_element_type=jnp.float32)
    expert_ids = jnp.arange(n_experts, dtype=jnp.int32)
    chosen = jnp.sum(
        jnp.where(routes[:, :, None] == expert_ids[None, None, :], logits[:, None, :], 0.0), axis=2
    )
    gates = jax.nn.softmax(chosen, axis=1)
    capacity = 16
    member = routes[:, :, None] == expert_ids[None, None, :]
    picks = jnp.any(member, axis=1).astype(jnp.float32)
    gate_of = jnp.sum(jnp.where(member, gates[:, :, None], 0.0), axis=1)
    earlier = (
        jnp.arange(token_index, dtype=jnp.int32)[:, None]
        > jnp.arange(token_index, dtype=jnp.int32)[None, :]
    ).astype(jnp.float32)
    rank = jnp.dot(earlier, picks, precision=lax.Precision.HIGHEST).astype(jnp.int32)
    place = jnp.arange(capacity, dtype=jnp.int32)
    select = (picks[None, :, :] > 0) & (rank[None, :, :] == place[:, None, None])
    select = jnp.transpose(select, (2, 0, 1))
    select2 = jnp.broadcast_to(select[:, None], (n_experts, 2, capacity, token_index)).reshape(
        2 * n_experts * capacity, token_index
    )
    outgoing = jnp.dot(
        select2.astype(jnp.bfloat16), normed, preferred_element_type=jnp.float32
    ).astype(jnp.bfloat16)
    outgoing = outgoing.reshape(2 * n_experts, capacity, D)
    rows = lax.all_to_all(outgoing, ("req", "exp"), split_axis=0, concat_axis=0, tiled=True)
    array_shape = rows.shape
    flat_rows = rows.reshape(-1, D)
    gate_part = jnp.dot(flat_rows, w_gate[0], preferred_element_type=jnp.float32)
    up_part = jnp.dot(flat_rows, w_up[0], preferred_element_type=jnp.float32)
    inner = (jax.nn.silu(gate_part) * up_part).astype(jnp.bfloat16)
    returned = lax.all_to_all(
        jnp.dot(inner, w_down[0], preferred_element_type=jnp.float32)
        .astype(jnp.bfloat16)
        .reshape(array_shape),
        ("req", "exp"),
        split_axis=0,
        concat_axis=0,
        tiled=True,
    ).reshape(2 * n_experts * capacity, D)
    weight = jnp.where(
        jnp.transpose(select, (2, 0, 1))[:, :, None, :], gate_of[:, :, None, None], 0.0
    )
    weight = jnp.broadcast_to(weight, (token_index, n_experts, 2, capacity)).reshape(
        token_index, 2 * n_experts * capacity
    )
    high = weight.astype(jnp.bfloat16)
    low = (weight - high.astype(jnp.float32)).astype(jnp.bfloat16)
    moe = jnp.dot(high, returned, preferred_element_type=jnp.float32) + jnp.dot(
        low, returned, preferred_element_type=jnp.float32
    )
    return (resid_f + moe).astype(jnp.bfloat16)


def solution(mesh):
    placed = (
        P(("req", "exp"), None),
        P(("req", "exp"), None),
        P(("req", "exp"), None),
        P("req", None),
        P("req", None, None),
        P("req", None, None),
        P(),
        P(),
        P(("req", "exp"), None),
        P(("req", "exp"), None, None),
        P(("req", "exp"), None, None),
        P(("req", "exp"), None, None),
    )
    return jax.shard_map(
        on_device, mesh=mesh, in_specs=placed, out_specs=P(("req", "exp"), None), check_vma=False
    )
```

profile of v0, /device:TPU:34, one launch (start us, length us, event | category | flops | bytes accessed | tf_op | source)
XLA Modules:
  0.0 531.8 jit_solution(14392213772407807917)
XLA Ops:
  7.4 0.0 copy-start
  7.4 0.0 all-gather.3.cloned.1.call-start
  7.4 1.9 copy.140
  9.3 0.0 all-gather.3.cloned.1.call-update
  9.3 0.8 reduce-window.4
  10.2 0.1 convert_reduce_fusion.1
  10.2 0.8 convert_reduce_fusion
  11.0 0.2 convolution_convert_fusion.3
  11.2 12.1 %all_gather.9 = bf16[1024,56]{0,1:T(8,128)(2,1)S(1)} all-gather(bf16[128,56]{0,1:T(8,128)(2,1)S(1)} %convolution_convert_fusion.3), channel_id=1, replica_groups=mesh['req'=8,'exp'=16] {'req'}, dimensions={0}, use_global_device_ids=true | all-gather | bytes 129024 | tf_op jit(solution)/shard_map/all_gather | solution.py:78
  23.4 0.2 bitcast_compare_fusion
  23.6 1.2 fusion.69
  24.8 0.2 copy.139
  25.1 16.3 %all-gather.3.cloned.1.call-done = bf16[1024,1280]{0,1:T(8,128)(2,1)} async-done(((bf16[128,1280]{0,1:T(8,128)(2,1)}), bf16[1024,1280]{0,1:T(8,128)(2,1)}) %all-gather.3.cloned.1.call-update) | async-done | bytes 2621456 | tf_op jit(solution)/shard_map/all_gather | solution.py:77
  41.4 16.3 %fusion = (f32[1024,2,5]{0,2,1:T(8,128)S(1)}, f32[2,896,1024,5]{2,1,3,0:T(8,128)}) fusion(pred[1024,896]{0,1:T(8,128)(4,1)S(1)} %bitcast_compare_fusion, bf16[896,2,128,1]{0,2,3,1:T(8,128)(2,1)S(1)} %bitcast.144, bf16[1024,2,5,128]{0,3,2,1:T(8,128)(2,1)} %bitcast.138), kind=kOutput, calls=%fused_computation.2 | convolution fusion | flops 2376325120 | bytes 40738816 | tf_op jit(solution)/shard_map/tgrd,kgd->tgrk/dot_general | solution.py:18
  57.7 0.4 broadcast_in_dim.146
  58.2 1.8 copy-done.1
  60.0 15.7 %fusion.4 = f32[1024,2,5]{0,2,1:T(8,128)S(1)} fusion(f32[2,896,1024,5]{2,1,3,0:T(8,128)} %get-tuple-element.20, f32[1024,896]{0,1:T(8,128)S(1)} %bitcast.133, f32[1024,2,5]{0,2,1:T(8,128)S(1)} %get-tuple-element.14, pred[1024,896]{0,1:T(8,128)(4,1)S(1)} %bitcast_compare_fusion), kind=kLoop, calls=%fused_computation.6 | loop fusion | flops 45864960 | bytes 41369600 | tf_op jit(solution)/shard_map/reduce_sum | solution.py:26
  75.7 0.6 copy.164
  76.3 4.0 all-to-all-start.2
  80.3 0.0 all-gather.5.cloned.1.call-start
  80.4 0.8 copy.146
  81.2 0.0 all-gather.5.cloned.1.call-update
  81.2 0.2 copy.155
  81.4 0.6 copy.144
  82.1 3.8 all-to-all-done.2
  85.8 3.3 all-to-all-start
  89.2 17.4 %bitcast_add_fusion = f32[1024,2,5,128]{3,0,2,1:T(8,128)S(1)} fusion(f32[1024,2,5]{0,2,1:T(8,128)S(1)} %get-tuple-element.13, bf16[896,2,128,1]{0,2,3,1:T(8,128)(2,1)S(1)} %bitcast.150, f32[2,896,1024,5]{2,1,3,0:T(8,128)} %get-tuple-element.20, f32[1024,896]{0,1:T(8,128)} %bitcast.134, f32[1024,2,5]{0,2,1:T(8,128)S(1)} %get-tuple-element.14, ...), kind=kOutput, calls=%fused_computation.21 | convolution fusion | flops 2395996160 | bytes 47071232 | tf_op jit(solution)/shard_map/tgrk,kgd->tgrd/dot_general | solution.py:27
  106.6 0.0 copy-start.9
  106.6 0.0 copy-start.7
  106.7 2.7 copy.158
  109.4 0.0 all-to-all-done
  109.4 5.0 all-to-all-start.1
  114.4 0.1 select_reduce_fusion.2
  114.4 0.0 copy-done.7
  114.5 0.1 convolution_convert_fusion.2
  114.6 0.1 fusion.47
  114.8 0.3 broadcast_compare_fusion
  115.1 0.0 copy-start.4
  115.1 15.4 %all-gather.5.cloned.1.call-done = bf16[2048,512]{0,1:T(8,128)(2,1)} async-done(((bf16[128,512]{0,1:T(8,128)(2,1)}), bf16[2048,512]{0,1:T(8,128)(2,1)}) %all-gather.5.cloned.1.call-update) | async-done | bytes 2097168 | tf_op jit(solution)/shard_map/all_gather | solution.py:127
  130.5 2.7 fusion.68
  133.2 5.8 %fusion.9 = (f32[128,2,5]{0,2,1:T(8,128)S(1)}, f32[2,2048,128,5]{2,1,3,0:T(8,128)}) fusion(pred[128,2048]{0,1:T(8,128)(4,1)S(1)} %get-tuple-element.17, bf16[2048,2,128,1]{0,2,3,1:T(8,128)(2,1)S(1)} %bitcast.141, bf16[128,2,5,128]{0,3,2,1:T(8,128)(2,1)S(1)} %bitcast.140), kind=kOutput, calls=%fused_computation.14 | convolution fusion | flops 678951680 | bytes 12129280 | tf_op jit(solution)/shard_map/tgrd,kgd->tgrk/dot_general | solution.py:18
  139.2 6.4 %fusion.13 = f32[128,2,5]{0,2,1:T(8,128)S(1)} fusion(f32[2,2048,128,5]{2,1,3,0:T(8,128)} %get-tuple-element.22, f32[128,2048]{0,1:T(8,128)S(1)} %get-tuple-element.18, f32[128,2,5]{0,2,1:T(8,128)S(1)} %copy.161, pred[128,2048]{0,1:T(8,128)(4,1)S(1)} %get-tuple-element.17), kind=kLoop, calls=%fused_computation.18 | loop fusion | flops 13105920 | bytes 11806720 | tf_op jit(solution)/shard_map/reduce_sum | solution.py:26
  145.7 29.6 %all-to-all-done.1 = f32[8,128,2,5,128]{4,1,3,2,0:T(8,128)} async-done(((f32[8,128,2,5,128]{4,1,3,2,0:T(8,128)}), f32[8,128,2,5,128]{4,1,3,2,0:T(8,128)}, u32[]{:S(2)}, u32[]{:S(2)}) %all-to-all-start.1) | async-done | bytes 5242912 | tf_op jit(solution)/shard_map/all_to_all | solution.py:114
  175.3 4.3 multiply_reduce_fusion
  179.6 2.2 copy.160
  181.8 7.9 %fusion.42 = bf16[128,2,5,128]{0,3,2,1:T(8,128)(2,1)S(1)} fusion(bf16[2048,2,128,1]{0,2,3,1:T(8,128)(2,1)} %bitcast.147, f32[2,2048,128,5]{2,1,3,0:T(8,128)} %get-tuple-element.22, f32[128,2048]{0,1:T(8,128)} %copy-done.4, f32[128,2,5]{0,2,1:T(8,128)S(1)} %copy.161, pred[128,2048]{0,1:T(8,128)(4,1)S(1)} %get-tuple-element.17, ...), kind=kOutput, calls=%fused_computation.49 | convolution fusion | flops 684851200 | bytes 13843456 | tf_op jit(solution)/shard_map/tgrk,kgd->tgrd/dot_general | solution.py:27
  189.7 1.0 fusion.25
  190.7 0.2 fusion.29
  191.0 0.1 broadcast_in_dim.166
  191.0 3.2 convolution_convert_fusion.1
  194.3 0.0 copy-start.8
  194.3 126.3 %all_to_all.25 = bf16[128,16,2560]{2,1,0:T(8,128)(2,1)S(1)} all-to-all(bf16[128,16,2560]{2,1,0:T(8,128)(2,1)S(1)} %bitcast.130), channel_id=1, replica_groups=mesh['req'=8,'exp'=16] {'req','exp'}, dimensions={0} | all-to-all | bytes 20971520 | tf_op jit(solution)/shard_map/all_to_all | solution.py:175
  320.5 3.8 copy-done.2
  324.4 10.2 %fusion.21 = f32[2048,768]{1,0:T(8,128)} fusion(bf16[2048,2560]{1,0:T(8,128)(2,1)S(1)} %bitcast.136, bf16[1,2560,768]{2,1,0:T(8,128)(2,1)S(1)} %copy-done.8), kind=kOutput, calls=%fused_computation.27 | convolution fusion | flops 8053063680 | bytes 20709376 | tf_op jit(solution)/shard_map/dot_general | solution.py:178
  334.5 28.9 %convolution_convert_fusion = bf16[2048,2560]{1,0:T(8,128)(2,1)} fusion(f32[2048,768]{1,0:T(8,128)} %fusion.21, bf16[2048,2560]{1,0:T(8,128)(2,1)} %bitcast.137, bf16[1,768,2560]{2,1,0:T(8,128)(2,1)} %param.23, bf16[1,2560,768]{2,1,0:T(8,128)(2,1)} %param.22), kind=kOutput, calls=%fused_computation.10 | convolution fusion | flops 16120807424 | bytes 35127296 | tf_op jit(solution)/shard_map/dot_general | solution.py:182
  363.5 6.7 %all-to-all-start.4 = ((bf16[128,16,2560]{2,1,0:T(8,128)(2,1)}), bf16[128,16,2560]{2,1,0:T(8,128)(2,1)}, u32[]{:S(2)}, u32[]{:S(2)}) async-start(bf16[128,16,2560]{2,1,0:T(8,128)(2,1)} %bitcast.135), calls=%async_computation.4 | async-start | bytes 20971520 | tf_op jit(solution)/shard_map/all_to_all | solution.py:181
  370.1 0.4 fusion.49
  370.7 0.1 select_convert_fusion
  370.8 0.1 fusion.45
  371.0 141.3 %all-to-all-done.4 = bf16[128,16,2560]{2,1,0:T(8,128)(2,1)} async-done(((bf16[128,16,2560]{2,1,0:T(8,128)(2,1)}), bf16[128,16,2560]{2,1,0:T(8,128)(2,1)}, u32[]{:S(2)}, u32[]{:S(2)}) %all-to-all-start.4) | async-done | bytes 10485792 | tf_op jit(solution)/shard_map/all_to_all | solution.py:181
  512.3 0.1 broadcast_in_dim.165
  512.3 5.5 %fusion.70 = f32[128,2560]{1,0:T(8,128)S(1)} fusion(bf16[128,2048]{0,1:T(8,128)(2,1)S(1)} %bitcast.143, bf16[2048,2560]{1,0:T(8,128)(2,1)} %bitcast.34), kind=kOutput, calls=%fused_computation.101 | convolution fusion | flops 1342177280 | bytes 12320768 | tf_op jit(solution)/shard_map/dot_general | solution.py:198
  517.9 0.1 broadcast_in_dim.167
  518.0 6.4 %fusion.24 = bf16[128,2560]{1,0:T(8,128)(2,1)} fusion(f32[128,2560]{1,0:T(8,128)S(1)} %fusion.70, bf16[128,2048]{0,1:T(8,128)(2,1)S(1)} %bitcast.142, bf16[2048,2560]{1,0:T(8,128)(2,1)} %bitcast.34, bf16[128,2560]{1,0:T(8,128)(2,1)S(1)} %fusion.25), kind=kOutput, calls=%fused_computation.32 | convolution fusion | flops 1343488000 | bytes 13631488 | tf_op jit(solution)/shard_map/dot_general | solution.py:198
  (41 shorter events, 0.4 us)
Async XLA Ops:
  7.4 362.8 %copy-start = (bf16[2560,64]{0,1:T(8,128)(2,1)S(1)}, bf16[2560,64]{0,1:T(8,128)(2,1)}, u32[]{:S(2)}) copy-start(bf16[2560,64]{0,1:T(8,128)(2,1)} %param.19) | copy-start | bytes 983044
  7.4 34.0 %all-gather.3.cloned.1.call-start = ((), (), s32[]{:S(2)}) async-start(), calls=%async_computation.5 | async-start | bytes 2949120 | tf_op jit(solution)/shard_map/all_gather | solution.py:77
  58.2 1.8 copy-start.1
  60.0 20.4 %copy-start.6 = (bf16[128,512]{1,0:T(8,128)(2,1)S(1)}, bf16[128,512]{1,0:T(8,128)(2,1)}, u32[]{:S(2)}) copy-start(bf16[128,512]{1,0:T(8,128)(2,1)} %param.14) | copy-start | bytes 393220
  76.3 9.5 %all-to-all-start.2 = ((f32[8,128,2,5]{1,2,3,0:T(2,128)}), f32[8,128,2,5]{1,2,3,0:T(2,128)S(1)}, u32[]{:S(2)}, u32[]{:S(2)}) async-start(f32[8,128,2,5]{1,2,3,0:T(2,128)} %copy.164), calls=%async_computation.2 | async-start | bytes 81920 | tf_op jit(solution)/shard_map/all_to_all | solution.py:107
  80.3 50.2 %all-gather.5.cloned.1.call-start = ((), (), s32[]{:S(2)}) async-start(), calls=%async_computation.6 | async-start | bytes 2228224 | tf_op jit(solution)/shard_map/all_gather | solution.py:127
  85.8 23.6 %all-to-all-start = ((f32[8,128,2,5]{1,2,3,0:T(2,128)}), f32[8,128,2,5]{1,2,3,0:T(2,128)S(1)}, u32[]{:S(2)}, u32[]{:S(2)}) async-start(f32[8,128,2,5]{1,2,3,0:T(2,128)} %copy.144), calls=%async_computation | async-start | bytes 81920 | tf_op jit(solution)/shard_map/all_to_all | solution.py:100
  106.6 7.7 %copy-start.9 = (s32[1,4]{1,0:T(1,128)S(1)}, s32[1,4]{1,0:T(1,128)}, u32[]{:S(2)}) copy-start(s32[1,4]{1,0:T(1,128)} %param.15) | copy-start | bytes 52
  106.6 7.8 %copy-start.7 = (s32[128,6]{0,1:T(8,128)S(1)}, s32[128,6]{0,1:T(8,128)}, u32[]{:S(2)}) copy-start(s32[128,6]{0,1:T(8,128)} %param.20) | copy-start | bytes 9220
  109.4 23.9 %copy-start.3 = (bf16[128,1280]{0,1:T(8,128)(2,1)S(1)}, bf16[128,1280]{0,1:T(8,128)(2,1)}, u32[]{:S(2)}) copy-start(bf16[128,1280]{0,1:T(8,128)(2,1)} %copy.140) | copy-start | bytes 983044
  109.4 65.9 %all-to-all-start.1 = ((f32[8,128,2,5,128]{4,1,3,2,0:T(8,128)}), f32[8,128,2,5,128]{4,1,3,2,0:T(8,128)}, u32[]{:S(2)}, u32[]{:S(2)}) async-start(f32[8,128,2,5,128]{4,1,3,2,0:T(8,128)} %copy.158), calls=%async_computation.1 | async-start | bytes 10485760 | tf_op jit(solution)/shard_map/all_to_all | solution.py:114
  115.1 24.1 %copy-start.4 = (f32[128,2048]{0,1:T(8,128)}, f32[128,2048]{0,1:T(8,128)S(1)}, u32[]{:S(2)}) copy-start(f32[128,2048]{0,1:T(8,128)S(1)} %get-tuple-element.18) | copy-start | bytes 3145732
  175.3 14.4 %slice-start = ((s8[6553600]{0:T(1024)(128)(4,1)}), s8[2359296]{0:T(1024)(128)(4,1)S(1)}, s32[]{:S(2)}) async-start(s8[6553600]{0:T(1024)(128)(4,1)} %bitcast.131), calls=%async_computation.7 | async-start | bytes 4718592
  181.8 7.9 %slice-start.1 = ((s8[6553600]{0:T(1024)(128)(4,1)}), s8[4194304]{0:T(1024)(128)(4,1)S(1)}, s32[]{:S(2)}) async-start(s8[6553600]{0:T(1024)(128)(4,1)} %bitcast.131), calls=%async_computation.8 | async-start | bytes 8388608
  181.8 7.9 %copy-start.5 = (bf16[128,2560]{1,0:T(8,128)(2,1)S(1)}, bf16[128,2560]{1,0:T(8,128)(2,1)}, u32[]{:S(2)}) copy-start(bf16[128,2560]{1,0:T(8,128)(2,1)} %param.12) | copy-start | bytes 1966084
  194.3 130.1 %copy-start.8 = (bf16[1,2560,768]{2,1,0:T(8,128)(2,1)S(1)}, bf16[1,2560,768]{2,1,0:T(8,128)(2,1)}, u32[]{:S(2)}) copy-start(bf16[1,2560,768]{2,1,0:T(8,128)(2,1)} %param.21) | copy-start | bytes 11796484
  320.5 3.8 copy-start.2
  363.5 148.8 %all-to-all-start.4 = ((bf16[128,16,2560]{2,1,0:T(8,128)(2,1)}), bf16[128,16,2560]{2,1,0:T(8,128)(2,1)}, u32[]{:S(2)}, u32[]{:S(2)}) async-start(bf16[128,16,2560]{2,1,0:T(8,128)(2,1)} %bitcast.135), calls=%async_computation.4 | async-start | bytes 20971520 | tf_op jit(solution)/shard_map/all_to_all | solution.py:181
Sparse Core Ops, SparseCore 0:
  9.9 31.4 all-gather.2
Sparse Core Ops, SparseCore 1:
  82.9 47.5 all-gather.4
where the time goes:
time: 533 us; the launch traced here: 532 us
  waiting for transfers between devices  206 us (39%)
  blocking collectives  138 us (26%)
  matrix products  104 us (20%)
  other arithmetic  29.7 us (6%)
  local copies, waits for them, and re-layouts  19.7 us (4%)
  starting transfers between devices  19 us (4%)
  between operations  15.2 us (3%)
    all_to_all x1, waiting for transfers between devices, on_device(): lax.all_to_all(jnp.dot(inner, w_down[0], preferred_element_type=jnp.float...  141 us
    all_to_all x1, blocking collectives, on_device(): lax.all_to_all(outgoing, ('req', 'exp'), split_axis=0, concat_axis=0, til...  126 us
    all_to_all x1, waiting for transfers between devices, on_device(): lax.all_to_all(summed_output.reshape(request_count, token_index, KEY_VALU...  29.6 us
    dot_general x1, matrix products, on_device(): jnp.dot(inner, w_down[0], preferred_element_type=jnp.float32)  28.9 us
    dot_general x2, matrix products, fold_scores(): jnp.einsum('tgrk,kgd->tgrd', expo.astype(jnp.bfloat16), value_rows, prefe...  25.3 us
    dot_general x2, matrix products, fold_scores(): jnp.einsum('tgrd,kgd->tgrk', query_matrix, key_rows, preferred_element_ty...  22.1 us
    reduce_sum x2, other arithmetic, fold_scores(): grand_total = decay * grand_total + jnp.sum(expo, axis=-1)  22.1 us
    all_gather x1, waiting for transfers between devices, on_device(): lax.all_gather(queries, 'req', axis=0, tiled=True)  16.3 us
  transfers between devices with their start and end apart: 6, of which 5 were waited for; matrix products, arithmetic and copies ran while one was open for 8% of the time, Pallas kernels for 0%

commit v1 on v0

--- a/solution.py
+++ b/solution.py
@@ -12,6 +12,11 @@
 PAGE_TOKENS = 128
 NEGATIVE_MASK = -1e30
 EPS = 1e-06
+
+
+def gather_from_all(value, axis, dim):
+    copies = jnp.concatenate([value] * lax.axis_size(axis), axis=dim)
+    return lax.all_to_all(copies, axis, dim, dim, tiled=True)
 
 
 def fold_scores(carry, query_matrix, key_rows, value_rows, weights):
@@ -75,7 +80,7 @@
     query_counts = jnp.dot(pick.astype(jnp.float32), counts, precision=lax.Precision.HIGHEST)
     query_total_set, every_count = (
         lax.all_gather(queries, "req", axis=0, tiled=True),
-        lax.all_gather(query_counts.astype(jnp.bfloat16), "req", axis=0, tiled=True),
+        gather_from_all(query_counts.astype(jnp.bfloat16), "req", 0),
     )
     query_total_count = query_total_set.shape[0]
     local = lax.dynamic_slice_in_dim(

time: 533 us -> 533 us (level)
  blocking collectives: 138 us -> 126 us
  waiting for transfers between devices: 206 us -> 213 us
    all_gather x1 -> x0, blocking collectives: 12.1 us -> none  [on_device(): lax.all_gather(query_counts.astype(jnp.bfloat16), 'req', axis=0, tiled=True)]
  transfers between devices with their start and end apart: 6 -> 7, of which waited for: 5 -> 6; matrix products, arithmetic and copies ran while one was open for 8% -> 8% of each run, Pallas kernels for 0% -> 0%
where the time goes in v1:
time: 533 us; the launch traced here: 532 us
  waiting for transfers between devices  213 us (40%)
  blocking collectives  126 us (24%)
  matrix products  104 us (20%)
  other arithmetic  29.7 us (6%)
  starting transfers between devices  23.4 us (4%)
  local copies, waits for them, and re-layouts  20.4 us (4%)
  between operations  15.3 us (3%)
    all_to_all x1, waiting for transfers between devices, on_device(): lax.all_to_all(jnp.dot(inner, w_down[0], preferred_element_type=jnp.float...  141 us
    all_to_all x1, blocking collectives, on_device(): lax.all_to_all(outgoing, ('req', 'exp'), split_axis=0, concat_axis=0, til...  126 us
    all_to_all x1, waiting for transfers between devices, on_device(): lax.all_to_all(summed_output.reshape(request_count, token_index, KEY_VALU...  29.6 us
    dot_general x1, matrix products, on_device(): jnp.dot(inner, w_down[0], preferred_element_type=jnp.float32)  28.9 us
    dot_general x2, matrix products, fold_scores(): jnp.einsum('tgrk,kgd->tgrd', expo.astype(jnp.bfloat16), value_rows, prefe...  25.3 us
    dot_general x2, matrix products, fold_scores(): jnp.einsum('tgrd,kgd->tgrk', query_matrix, key_rows, preferred_element_ty...  22.1 us
    reduce_sum x2, other arithmetic, fold_scores(): grand_total = decay * grand_total + jnp.sum(expo, axis=-1)  22.1 us
    all_gather x1, waiting for transfers between devices, on_device(): lax.all_gather(queries, 'req', axis=0, tiled=True)  18.6 us
  transfers between devices with their start and end apart: 7, of which 6 were waited for; matrix products, arithmetic and copies ran while one was open for 8% of the time, Pallas kernels for 0%

profile of v1, /device:TPU:34, one launch (start us, length us, event | category | flops | bytes accessed | tf_op | source)
XLA Modules:
  0.0 531.8 jit_solution(5143239296382281209)
XLA Ops:
  7.4 0.0 copy-start
  7.4 1.9 copy.176
  9.3 0.0 all-gather.3.cloned.1.call-update
  9.3 0.8 reduce-window.4
  10.2 0.1 convert_reduce_fusion.1
  10.2 0.8 convert_reduce_fusion
  11.0 0.2 constant_dynamic-update-slice_fusion.7
  11.3 0.7 copy_bitcast_fusion.1
  12.0 4.5 all-to-all-start
  16.5 1.2 fusion.69
  17.7 0.2 copy.175
  17.9 4.5 all-to-all-done
  22.5 0.2 bitcast_compare_fusion
  22.7 18.6 %all-gather.3.cloned.1.call-done = bf16[1024,1280]{0,1:T(8,128)(2,1)} async-done(((bf16[128,1280]{0,1:T(8,128)(2,1)}), bf16[1024,1280]{0,1:T(8,128)(2,1)}) %all-gather.3.cloned.1.call-update) | async-done | bytes 2621456 | tf_op jit(solution)/shard_map/all_gather | solution.py:82
  41.4 16.3 %fusion = (f32[1024,2,5]{0,2,1:T(8,128)S(1)}, f32[2,896,1024,5]{2,1,3,0:T(8,128)}) fusion(pred[1024,896]{0,1:T(8,128)(4,1)S(1)} %bitcast_compare_fusion, bf16[896,2,128,1]{0,2,3,1:T(8,128)(2,1)S(1)} %bitcast.154, bf16[1024,2,5,128]{0,3,2,1:T(8,128)(2,1)} %bitcast.148), kind=kOutput, calls=%fused_computation.2 | convolution fusion | flops 2376325120 | bytes 40738816 | tf_op jit(solution)/shard_map/tgrd,kgd->tgrk/dot_general | solution.py:23
  57.7 0.4 broadcast_in_dim.146
  58.2 1.8 copy-done.1
  60.0 15.7 %fusion.4 = f32[1024,2,5]{0,2,1:T(8,128)S(1)} fusion(f32[2,896,1024,5]{2,1,3,0:T(8,128)} %get-tuple-element.22, f32[1024,896]{0,1:T(8,128)S(1)} %bitcast.143, f32[1024,2,5]{0,2,1:T(8,128)S(1)} %get-tuple-element.14, pred[1024,896]{0,1:T(8,128)(4,1)S(1)} %bitcast_compare_fusion), kind=kLoop, calls=%fused_computation.6 | loop fusion | flops 45864960 | bytes 41369600 | tf_op jit(solution)/shard_map/reduce_sum | solution.py:31
  75.7 0.6 copy.200
  76.3 4.0 all-to-all-start.3
  80.3 0.0 all-gather.5.cloned.1.call-start
  80.4 0.8 copy.182
  81.2 0.0 all-gather.5.cloned.1.call-update
  81.2 0.2 copy.191
  81.4 0.6 copy.180
  82.1 3.8 all-to-all-done.3
  85.8 3.3 all-to-all-start.1
  89.2 17.4 %bitcast_add_fusion = f32[1024,2,5,128]{3,0,2,1:T(8,128)S(1)} fusion(f32[1024,2,5]{0,2,1:T(8,128)S(1)} %get-tuple-element.13, bf16[896,2,128,1]{0,2,3,1:T(8,128)(2,1)S(1)} %bitcast.160, f32[2,896,1024,5]{2,1,3,0:T(8,128)} %get-tuple-element.22, f32[1024,896]{0,1:T(8,128)} %bitcast.144, f32[1024,2,5]{0,2,1:T(8,128)S(1)} %get-tuple-element.14, ...), kind=kOutput, calls=%fused_computation.21 | convolution fusion | flops 2395996160 | bytes 47071232 | tf_op jit(solution)/shard_map/tgrk,kgd->tgrd/dot_general | solution.py:32
  106.6 0.0 copy-start.9
  106.6 0.0 copy-start.7
  106.7 2.7 copy.194
  109.4 0.0 all-to-all-done.1
  109.4 5.0 all-to-all-start.2
  114.4 0.1 select_reduce_fusion.2
  114.4 0.0 copy-done.7
  114.5 0.1 convolution_convert_fusion.2
  114.6 0.1 fusion.47
  114.8 0.3 broadcast_compare_fusion
  115.1 15.4 %all-gather.5.cloned.1.call-done = bf16[2048,512]{0,1:T(8,128)(2,1)} async-done(((bf16[128,512]{0,1:T(8,128)(2,1)}), bf16[2048,512]{0,1:T(8,128)(2,1)}) %all-gather.5.cloned.1.call-update) | async-done | bytes 2097168 | tf_op jit(solution)/shard_map/all_gather | solution.py:132
  130.5 2.7 fusion.68
  133.2 5.8 %fusion.9 = (f32[128,2,5]{0,2,1:T(8,128)S(1)}, f32[2,2048,128,5]{2,1,3,0:T(8,128)}) fusion(pred[128,2048]{0,1:T(8,128)(4,1)S(1)} %get-tuple-element.17, bf16[2048,2,128,1]{0,2,3,1:T(8,128)(2,1)S(1)} %bitcast.151, bf16[128,2,5,128]{0,3,2,1:T(8,128)(2,1)S(1)} %bitcast.150), kind=kOutput, calls=%fused_computation.14 | convolution fusion | flops 678951680 | bytes 12129280 | tf_op jit(solution)/shard_map/tgrd,kgd->tgrk/dot_general | solution.py:23
  139.2 6.4 %fusion.13 = f32[128,2,5]{0,2,1:T(8,128)S(1)} fusion(f32[2,2048,128,5]{2,1,3,0:T(8,128)} %get-tuple-element.24, f32[128,2048]{0,1:T(8,128)S(1)} %get-tuple-element.18, f32[128,2,5]{0,2,1:T(8,128)S(1)} %copy.197, pred[128,2048]{0,1:T(8,128)(4,1)S(1)} %get-tuple-element.17), kind=kLoop, calls=%fused_computation.18 | loop fusion | flops 13105920 | bytes 11806720 | tf_op jit(solution)/shard_map/reduce_sum | solution.py:31
  145.7 29.6 %all-to-all-done.2 = f32[8,128,2,5,128]{4,1,3,2,0:T(8,128)} async-done(((f32[8,128,2,5,128]{4,1,3,2,0:T(8,128)}), f32[8,128,2,5,128]{4,1,3,2,0:T(8,128)}, u32[]{:S(2)}, u32[]{:S(2)}) %all-to-all-start.2) | async-done | bytes 5242912 | tf_op jit(solution)/shard_map/all_to_all | solution.py:119
  175.3 4.3 multiply_reduce_fusion
  179.6 2.2 copy.196
  181.8 7.9 %fusion.42 = bf16[128,2,5,128]{0,3,2,1:T(8,128)(2,1)S(1)} fusion(bf16[2048,2,128,1]{0,2,3,1:T(8,128)(2,1)} %bitcast.157, f32[2,2048,128,5]{2,1,3,0:T(8,128)} %get-tuple-element.24, f32[128,2048]{0,1:T(8,128)} %copy-done.4, f32[128,2,5]{0,2,1:T(8,128)S(1)} %copy.197, pred[128,2048]{0,1:T(8,128)(4,1)S(1)} %get-tuple-element.17, ...), kind=kOutput, calls=%fused_computation.49 | convolution fusion | flops 684851200 | bytes 13843456 | tf_op jit(solution)/shard_map/tgrk,kgd->tgrd/dot_general | solution.py:32
  189.7 1.0 fusion.25
  190.7 0.2 fusion.29
  191.0 0.1 broadcast_in_dim.166
  191.0 3.2 convolution_convert_fusion.1
  194.3 0.0 copy-start.8
  194.3 126.3 %all_to_all.37 = bf16[128,16,2560]{2,1,0:T(8,128)(2,1)S(1)} all-to-all(bf16[128,16,2560]{2,1,0:T(8,128)(2,1)S(1)} %bitcast.140), channel_id=1, replica_groups=mesh['req'=8,'exp'=16] {'req','exp'}, dimensions={0} | all-to-all | bytes 20971520 | tf_op jit(solution)/shard_map/all_to_all | solution.py:180
  320.5 3.8 copy-done.2
  324.4 10.2 %fusion.21 = f32[2048,768]{1,0:T(8,128)} fusion(bf16[2048,2560]{1,0:T(8,128)(2,1)S(1)} %bitcast.146, bf16[1,2560,768]{2,1,0:T(8,128)(2,1)S(1)} %copy-done.8), kind=kOutput, calls=%fused_computation.27 | convolution fusion | flops 8053063680 | bytes 20709376 | tf_op jit(solution)/shard_map/dot_general | solution.py:183
  334.5 28.9 %convolution_convert_fusion = bf16[2048,2560]{1,0:T(8,128)(2,1)} fusion(f32[2048,768]{1,0:T(8,128)} %fusion.21, bf16[2048,2560]{1,0:T(8,128)(2,1)} %bitcast.147, bf16[1,768,2560]{2,1,0:T(8,128)(2,1)} %param.23, bf16[1,2560,768]{2,1,0:T(8,128)(2,1)} %param.22), kind=kOutput, calls=%fused_computation.10 | convolution fusion | flops 16120807424 | bytes 35127296 | tf_op jit(solution)/shard_map/dot_general | solution.py:187
  363.5 6.7 %all-to-all-start.5 = ((bf16[128,16,2560]{2,1,0:T(8,128)(2,1)}), bf16[128,16,2560]{2,1,0:T(8,128)(2,1)}, u32[]{:S(2)}, u32[]{:S(2)}) async-start(bf16[128,16,2560]{2,1,0:T(8,128)(2,1)} %bitcast.145), calls=%async_computation.5 | async-start | bytes 20971520 | tf_op jit(solution)/shard_map/all_to_all | solution.py:186
  370.1 0.4 fusion.49
  370.7 0.1 select_convert_fusion
  370.8 0.1 fusion.45
  371.0 141.3 %all-to-all-done.5 = bf16[128,16,2560]{2,1,0:T(8,128)(2,1)} async-done(((bf16[128,16,2560]{2,1,0:T(8,128)(2,1)}), bf16[128,16,2560]{2,1,0:T(8,128)(2,1)}, u32[]{:S(2)}, u32[]{:S(2)}) %all-to-all-start.5) | async-done | bytes 10485792 | tf_op jit(solution)/shard_map/all_to_all | solution.py:186
  512.3 0.1 broadcast_in_dim.165
  512.3 5.5 %fusion.70 = f32[128,2560]{1,0:T(8,128)S(1)} fusion(bf16[128,2048]{0,1:T(8,128)(2,1)S(1)} %bitcast.153, bf16[2048,2560]{1,0:T(8,128)(2,1)} %bitcast.34), kind=kOutput, calls=%fused_computation.111 | convolution fusion | flops 1342177280 | bytes 12320768 | tf_op jit(solution)/shard_map/dot_general | solution.py:203
  517.9 0.1 broadcast_in_dim.167
  518.0 6.4 %fusion.24 = bf16[128,2560]{1,0:T(8,128)(2,1)} fusion(f32[128,2560]{1,0:T(8,128)S(1)} %fusion.70, bf16[128,2048]{0,1:T(8,128)(2,1)S(1)} %bitcast.152, bf16[2048,2560]{1,0:T(8,128)(2,1)} %bitcast.34, bf16[128,2560]{1,0:T(8,128)(2,1)S(1)} %fusion.25), kind=kOutput, calls=%fused_computation.32 | convolution fusion | flops 1343488000 | bytes 13631488 | tf_op jit(solution)/shard_map/dot_general | solution.py:203
  (51 shorter events, 0.5 us)
Async XLA Ops:
  7.4 362.8 %copy-start = (bf16[2560,64]{0,1:T(8,128)(2,1)S(1)}, bf16[2560,64]{0,1:T(8,128)(2,1)}, u32[]{:S(2)}) copy-start(bf16[2560,64]{0,1:T(8,128)(2,1)} %param.19) | copy-start | bytes 983044
  7.4 34.0 %all-gather.3.cloned.1.call-start = ((), (), s32[]{:S(2)}) async-start(), calls=%async_computation.6 | async-start | bytes 2949120 | tf_op jit(solution)/shard_map/all_gather | solution.py:82
  12.0 10.4 %all-to-all-start = ((bf16[8,128,56]{1,2,0:T(8,128)(2,1)}), bf16[8,128,56]{1,2,0:T(8,128)(2,1)S(1)}, u32[]{:S(2)}, u32[]{:S(2)}) async-start(bf16[8,128,56]{1,2,0:T(8,128)(2,1)} %copy_bitcast_fusion.1), calls=%async_computation | async-start | bytes 229376 | tf_op jit(solution)/shard_map/all_to_all | solution.py:19
  58.2 1.8 copy-start.1
  60.0 20.4 %copy-start.6 = (bf16[128,512]{1,0:T(8,128)(2,1)S(1)}, bf16[128,512]{1,0:T(8,128)(2,1)}, u32[]{:S(2)}) copy-start(bf16[128,512]{1,0:T(8,128)(2,1)} %param.14) | copy-start | bytes 393220
  76.3 9.5 %all-to-all-start.3 = ((f32[8,128,2,5]{1,2,3,0:T(2,128)}), f32[8,128,2,5]{1,2,3,0:T(2,128)S(1)}, u32[]{:S(2)}, u32[]{:S(2)}) async-start(f32[8,128,2,5]{1,2,3,0:T(2,128)} %copy.200), calls=%async_computation.3 | async-start | bytes 81920 | tf_op jit(solution)/shard_map/all_to_all | solution.py:112
  80.3 50.2 %all-gather.5.cloned.1.call-start = ((), (), s32[]{:S(2)}) async-start(), calls=%async_computation.7 | async-start | bytes 2228224 | tf_op jit(solution)/shard_map/all_gather | solution.py:132
  85.8 23.6 %all-to-all-start.1 = ((f32[8,128,2,5]{1,2,3,0:T(2,128)}), f32[8,128,2,5]{1,2,3,0:T(2,128)S(1)}, u32[]{:S(2)}, u32[]{:S(2)}) async-start(f32[8,128,2,5]{1,2,3,0:T(2,128)} %copy.180), calls=%async_computation.1 | async-start | bytes 81920 | tf_op jit(solution)/shard_map/all_to_all | solution.py:105
  106.6 7.7 %copy-start.9 = (s32[1,4]{1,0:T(1,128)S(1)}, s32[1,4]{1,0:T(1,128)}, u32[]{:S(2)}) copy-start(s32[1,4]{1,0:T(1,128)} %param.15) | copy-start | bytes 52
  106.6 7.8 %copy-start.7 = (s32[128,6]{0,1:T(8,128)S(1)}, s32[128,6]{0,1:T(8,128)}, u32[]{:S(2)}) copy-start(s32[128,6]{0,1:T(8,128)} %param.20) | copy-start | bytes 9220
  109.4 23.9 %copy-start.3 = (bf16[128,1280]{0,1:T(8,128)(2,1)S(1)}, bf16[128,1280]{0,1:T(8,128)(2,1)}, u32[]{:S(2)}) copy-start(bf16[128,1280]{0,1:T(8,128)(2,1)} %copy.176) | copy-start | bytes 983044
  109.4 65.9 %all-to-all-start.2 = ((f32[8,128,2,5,128]{4,1,3,2,0:T(8,128)}), f32[8,128,2,5,128]{4,1,3,2,0:T(8,128)}, u32[]{:S(2)}, u32[]{:S(2)}) async-start(f32[8,128,2,5,128]{4,1,3,2,0:T(8,128)} %copy.194), calls=%async_computation.2 | async-start | bytes 10485760 | tf_op jit(solution)/shard_map/all_to_all | solution.py:119
  115.1 24.1 %copy-start.4 = (f32[128,2048]{0,1:T(8,128)}, f32[128,2048]{0,1:T(8,128)S(1)}, u32[]{:S(2)}) copy-start(f32[128,2048]{0,1:T(8,128)S(1)} %get-tuple-element.18) | copy-start | bytes 3145732
  175.3 14.4 %slice-start = ((s8[6553600]{0:T(1024)(128)(4,1)}), s8[2359296]{0:T(1024)(128)(4,1)S(1)}, s32[]{:S(2)}) async-start(s8[6553600]{0:T(1024)(128)(4,1)} %bitcast.141), calls=%async_computation.8 | async-start | bytes 4718592
  181.8 7.9 %slice-start.1 = ((s8[6553600]{0:T(1024)(128)(4,1)}), s8[4194304]{0:T(1024)(128)(4,1)S(1)}, s32[]{:S(2)}) async-start(s8[6553600]{0:T(1024)(128)(4,1)} %bitcast.141), calls=%async_computation.9 | async-start | bytes 8388608
  181.8 7.9 %copy-start.5 = (bf16[128,2560]{1,0:T(8,128)(2,1)S(1)}, bf16[128,2560]{1,0:T(8,128)(2,1)}, u32[]{:S(2)}) copy-start(bf16[128,2560]{1,0:T(8,128)(2,1)} %param.12) | copy-start | bytes 1966084
  194.3 130.1 %copy-start.8 = (bf16[1,2560,768]{2,1,0:T(8,128)(2,1)S(1)}, bf16[1,2560,768]{2,1,0:T(8,128)(2,1)}, u32[]{:S(2)}) copy-start(bf16[1,2560,768]{2,1,0:T(8,128)(2,1)} %param.21) | copy-start | bytes 11796484
  320.5 3.8 copy-start.2
  363.5 148.8 %all-to-all-start.5 = ((bf16[128,16,2560]{2,1,0:T(8,128)(2,1)}), bf16[128,16,2560]{2,1,0:T(8,128)(2,1)}, u32[]{:S(2)}, u32[]{:S(2)}) async-start(bf16[128,16,2560]{2,1,0:T(8,128)(2,1)} %bitcast.145), calls=%async_computation.5 | async-start | bytes 20971520 | tf_op jit(solution)/shard_map/all_to_all | solution.py:186
Sparse Core Ops, SparseCore 0:
  9.9 31.4 all-gather.2
Sparse Core Ops, SparseCore 1:
  82.9 47.5 all-gather.4
